TPU v7x, 32 devices: a whole 2x2x4 slice. The times are simulated.
32 devices in a mesh: seq: 8 (over y, x, core), panel: 4 (over z).
Axes of the slice: x: 2, y: 2, z: 4, core: 2. Of those that a mesh axis runs over, the one named last changes fastest.
Arguments:
- tokens: bfloat16 [2048, 1024], P('seq', 'panel'), may hold values from -6 to 6
- cotangent: bfloat16 [2048, 1024], P('seq', 'panel'), may hold values from -6 to 6
- in_weight: bfloat16 [3, 1024, 1024], P(None, None, 'panel'), may hold values from -0.1875 to 0.1875
- short_kernel: float32 [3, 3, 1024], P(None, None, 'panel'), may hold values from -1 to 1
- skip_gain: float32 [1024], P('panel'), may hold values from 0.5 to 1.5
- long_filter: float32 [2048, 1024], P('seq', 'panel'), may hold values from -1.25 to 1.25
- out_weight: bfloat16 [1024, 1024], P('panel'), may hold values from -0.1875 to 0.1875
Outputs:
- block_out: bfloat16 [2048, 1024], P('seq', 'panel')
- token_grad: bfloat16 [2048, 1024], P('seq', 'panel')
All inputs are finite; a program needn't handle non-finite values.
Results may differ from a plain program's by a relative error of at most 0.007.
Values may be sent and summed in bfloat16 or wider, within the bound.
No kernel may reach another device: no remote copies, remote signals or barrier semaphores. Data moves between devices by JAX's collectives and lax.ppermute only.
A program may use at most 64 MiB of HBM per device.

v0:
```python
import math
import jax
import jax.numpy as jnp
import numpy as np
from jax import lax
from jax.sharding import PartitionSpec as P

HIGHEST = lax.Precision.HIGHEST
STAGE_A_PRECISION = lax.Precision.HIGH
STAGE_B_PRECISION = lax.Precision.HIGH
WIRE = jnp.bfloat16


def shifted(value, axis, steps):
    count = lax.axis_size(axis)
    initial, last = (max(0, -steps), min(count, count - steps))
    return lax.ppermute(value, axis, [(source, source + steps) for source in range(initial, last)])


def panel_parts(value):
    count = lax.axis_size("panel")
    me = lax.axis_index("panel")
    parts = [(value, me)]
    for k in range(1, count):
        moved = lax.ppermute(value, "panel", [(i, (i + k) % count) for i in range(count)])
        parts.append((moved, (me + count - k) % count))
    return parts


def panel_reduce_scatter(block_of):
    count = lax.axis_size("panel")
    me = lax.axis_index("panel")
    total = block_of(me)
    for k in range(1, count):
        sent = block_of((me + k) % count).astype(jnp.bfloat16)
        total = total + lax.ppermute(
            sent, "panel", [(i, (i + k) % count) for i in range(count)]
        ).astype(jnp.float32)
    return total.astype(jnp.bfloat16)


def phase(numer, period):
    return 2.0 * math.pi / period * (numer % period).astype(jnp.float32)


def transform_tables(shard_count, row_count):
    length = shard_count * row_count
    branch = jnp.arange(2, dtype=jnp.int32)
    shard = jnp.arange(shard_count, dtype=jnp.int32)
    row = jnp.arange(row_count, dtype=jnp.int32)
    small_shard, small_row = (np.arange(shard_count), np.arange(row_count))
    small_branch = np.arange(2)
    theta = (
        -2.0
        * math.pi
        / (2 * shard_count)
        * (
            (
                (2 * small_shard[:, None] * small_shard[None, :])[None]
                + small_branch[:, None, None] * small_shard[None, None, :]
            )
            % (2 * shard_count)
        )
    )
    stage_a_np = np.stack([np.cos(theta), np.sin(theta)], axis=1)
    stage_a = jnp.asarray(stage_a_np, dtype=jnp.float32)
    phi = (
        -2.0
        * math.pi
        / (2 * length)
        * (
            (
                (2 * small_shard[:, None] * small_row[None, :])[None]
                + small_branch[:, None, None] * small_row[None, :][None]
            )
            % (2 * length)
        )
    )
    twiddle = (jnp.asarray(np.cos(phi), jnp.float32), jnp.asarray(np.sin(phi), jnp.float32))
    psi = -phase(row[:, None] * row[None, :], row_count)
    cos_b, sin_b = (jnp.cos(psi), jnp.sin(psi))
    stage_b = jnp.stack([jnp.stack([cos_b, sin_b], axis=1), jnp.stack([-sin_b, cos_b], axis=1)])
    stage_a_inv = jnp.asarray(stage_a_np * (0.5 / length), dtype=jnp.float32)
    return (stage_a, twiddle, stage_b, stage_a_inv)


def complex_scale(value, cos_part, sin_part, axis):
    real_part = lax.index_in_dim(value, 0, axis, keepdims=False)
    imag_part = lax.index_in_dim(value, 1, axis, keepdims=False)
    return jnp.stack(
        [real_part * cos_part - imag_part * sin_part, real_part * sin_part + imag_part * cos_part],
        axis=axis,
    )


def to_columns(rows, wire=jnp.float32):
    shard_count = lax.axis_size("seq")
    batch, row_count, _ = rows.shape
    columns = lax.all_to_all(
        jnp.swapaxes(rows, 1, 2).astype(wire), "seq", split_axis=1, concat_axis=2, tiled=True
    ).astype(jnp.float32)
    return columns.reshape(batch, columns.shape[1], shard_count, row_count)


def to_rows(columns, wire=jnp.float32):
    batch, chan_count, shard_count, row_count = columns.shape
    rows = lax.all_to_all(
        columns.astype(wire), "seq", split_axis=2, concat_axis=1, tiled=True
    ).astype(jnp.float32)
    return jnp.swapaxes(rows.reshape(batch, shard_count * chan_count, row_count), 1, 2)


def forward_spectrum(columns, tables):
    stage_a, twiddle, stage_b, _ = tables
    spread = jnp.einsum("erkp,bcpm->bcerkm", stage_a, columns, precision=STAGE_A_PRECISION)
    spread = complex_scale(spread, twiddle[0], twiddle[1], 3)
    return jnp.einsum("bcerkm,rmsq->bceskq", spread, stage_b, precision=STAGE_B_PRECISION)


def inverse_spectrum(spectrum, tables):
    _, twiddle, stage_b, stage_a_inv = tables
    spread = jnp.einsum("bceskq,rmsq->bcerkm", spectrum, stage_b, precision=STAGE_B_PRECISION)
    spread = complex_scale(spread, twiddle[0], -twiddle[1], 3)
    return jnp.einsum("erkp,bcerkm->bcpm", stage_a_inv, spread, precision=STAGE_A_PRECISION)


def local(tokens, cotangent, in_weight, short_kernel, skip_gain, long_filter, out_weight):
    row_count = tokens.shape[0]
    tap_count = short_kernel.shape[0]
    shard_count = lax.axis_size("seq")
    tables = transform_tables(shard_count, row_count)
    filt_spec = forward_spectrum(to_columns(long_filter[None]), tables)
    width = tokens.shape[1]
    projected = 0.0
    for part, source in panel_parts(tokens):
        projected = projected + jnp.einsum(
            "td,jdc->jtc",
            part,
            lax.dynamic_slice_in_dim(in_weight, source * width, width, axis=1),
            preferred_element_type=jnp.float32,
        )
    grad_gated = 0.0
    for part, source in panel_parts(cotangent):
        grad_gated = grad_gated + lax.dot_general(
            part,
            lax.dynamic_slice_in_dim(out_weight, source * width, width, axis=1),
            (((1,), (1,)), ((), ())),
            preferred_element_type=jnp.float32,
        )
    projected = projected.astype(jnp.bfloat16)
    before = shifted(projected[:, row_count - (tap_count - 1) :, :], "seq", 1)
    extended = jnp.concatenate([before, projected], axis=1).astype(jnp.float32)
    filtered = short_kernel[0][:, None, :] * extended[:, tap_count - 1 :, :]
    for tap_index in range(1, tap_count):
        filtered = (
            filtered
            + short_kernel[tap_index][:, None, :]
            * extended[:, tap_count - 1 - tap_index : tap_count - 1 - tap_index + row_count, :]
        )
    gate_out, gate_in, value_path = (filtered[0], filtered[1], filtered[2])
    signal = value_path * gate_in
    grad_state = grad_gated * gate_out
    spectra = forward_spectrum(to_columns(jnp.stack([signal, grad_state]), WIRE), tables)
    filt_real, filt_imag = (filt_spec[:, :, :, 0], filt_spec[:, :, :, 1])
    sig_real, sig_imag = (spectra[0:1, :, :, 0], spectra[0:1, :, :, 1])
    grad_real, grad_imag = (spectra[1:2, :, :, 0], spectra[1:2, :, :, 1])
    product = jnp.concatenate(
        [
            jnp.stack(
                [
                    sig_real * filt_real - sig_imag * filt_imag,
                    sig_real * filt_imag + sig_imag * filt_real,
                ],
                axis=3,
            ),
            jnp.stack(
                [
                    grad_real * filt_real + grad_imag * filt_imag,
                    grad_imag * filt_real - grad_real * filt_imag,
                ],
                axis=3,
            ),
        ]
    )
    convolved = to_rows(inverse_spectrum(product, tables), WIRE)
    conv_state = convolved[0] + skip_gain[None, :] * signal
    grad_signal = convolved[1] + skip_gain[None, :] * grad_state
    gated_state = (conv_state * gate_out).astype(jnp.bfloat16)
    block_out = panel_reduce_scatter(
        lambda dest: jnp.dot(
            gated_state,
            lax.dynamic_slice_in_dim(out_weight, dest * width, width, axis=1),
            preferred_element_type=jnp.float32,
        )
    )
    grad_gate_out = grad_gated * conv_state
    grad_value = grad_signal * gate_in
    grad_gate_in = grad_signal * value_path
    upstream = jnp.stack([grad_gate_out, grad_gate_in, grad_value])
    after_rim = shifted(upstream[:, : tap_count - 1, :], "seq", -1)
    widened = jnp.concatenate([upstream, after_rim], axis=1)
    grad_projected = short_kernel[0][:, None, :] * widened[:, :row_count, :]
    for tap_index in range(1, tap_count):
        grad_projected = (
            grad_projected
            + short_kernel[tap_index][:, None, :] * widened[:, tap_index : tap_index + row_count, :]
        )
    grad_projected = grad_projected.astype(jnp.bfloat16)
    token_grad = panel_reduce_scatter(
        lambda dest: jnp.einsum(
            "jtc,jdc->td",
            grad_projected,
            lax.dynamic_slice_in_dim(in_weight, dest * width, width, axis=1),
            preferred_element_type=jnp.float32,
        )
    )
    return (block_out, token_grad)


def solution(mesh):
    placed = (
        P("seq", "panel"),
        P("seq", "panel"),
        P(None, None, "panel"),
        P(None, None, "panel"),
        P("panel"),
        P("seq", "panel"),
        P("panel", None),
    )
    return jax.shard_map(
        local,
        mesh=mesh,
        in_specs=placed,
        out_specs=(P("seq", "panel"), P("seq", "panel")),
        check_vma=False,
    )
```

profile of v0, /device:TPU:9, one launch (start us, length us, event | category | flops | bytes accessed | tf_op | source)
XLA Modules:
  0.0 95.5 jit_solution(1160381794692749451)
XLA Ops:
  0.7 1.3 %collective-permute-start = (bf16[256,256]{1,0:T(8,128)(2,1)}, bf16[256,256]{1,0:T(8,128)(2,1)}, u32[]{:S(2)}, u32[]{:S(2)}) collective-permute-start(bf16[256,256]{1,0:T(8,128)(2,1)} %param.11), channel_id=1, source_target_pairs={{0,1},{1,2},{2,3},{3,0},{4,5},{5,6},{6,7},{7,4},{8,9},{9,10},{10,1... | collective-permute-start | bytes 393224 | tf_op jit(solution)/shard_map/ppermute | solution.py:25
  2.2 2.3 %collective-permute-start.1 = (bf16[256,256]{1,0:T(8,128)(2,1)}, bf16[256,256]{1,0:T(8,128)(2,1)}, u32[]{:S(2)}, u32[]{:S(2)}) collective-permute-start(bf16[256,256]{1,0:T(8,128)(2,1)} %param.11), channel_id=1, source_target_pairs={{0,2},{1,3},{2,0},{3,1},{4,6},{5,7},{6,4},{7,5},{8,10},{9,11},{10,... | collective-permute-start | bytes 393224 | tf_op jit(solution)/shard_map/ppermute | solution.py:25
  4.5 1.0 %collective-permute-start.4 = (bf16[256,256]{1,0:T(8,128)(2,1)}, bf16[256,256]{1,0:T(8,128)(2,1)}, u32[]{:S(2)}, u32[]{:S(2)}) collective-permute-start(bf16[256,256]{1,0:T(8,128)(2,1)} %param.12), channel_id=1, source_target_pairs={{0,1},{1,2},{2,3},{3,0},{4,5},{5,6},{6,7},{7,4},{8,9},{9,10},{10,1... | collective-permute-start | bytes 393224 | tf_op jit(solution)/shard_map/ppermute | solution.py:25
  5.5 0.5 collective-permute-start.6
  6.0 1.8 %copy.64 = f32[1,256,256]{1,0,2:T(1,128)} copy(f32[1,256,256]{2,1,0:T(8,128)} %bitcast.216) | data formatting | bytes 524288 | tf_op jit(solution)/shard_map/broadcast_in_dim | solution.py:132
  7.7 5.8 %all-to-all-start.1 = ((f32[1,256,256]{2,0,1:T(1,128)}), f32[1,256,256]{2,0,1:T(1,128)S(1)}, u32[]{:S(2)}, u32[]{:S(2)}) async-start(f32[1,256,256]{2,0,1:T(1,128)} %bitcast.34), calls=%async_computation.1 | async-start | bytes 524288 | tf_op jit(solution)/shard_map/all_to_all | solution.py:99
  13.5 1.0 %fusion.88 = f32[256,1,256]{2,0,1:T(8,128)S(1)} fusion(), kind=kLoop, calls=%fused_computation.124 | loop fusion | flops 1048576 | bytes 262144 | tf_op jit(solution)/shard_map/neg | solution.py:82
  14.5 1.0 %fusion.86 = (f32[256,1,256]{2,0,1:T(8,128)S(1)}, f32[256,1,256]{2,0,1:T(8,128)S(1)}) fusion(), kind=kLoop, calls=%fused_computation.122 | loop fusion | flops 983040 | bytes 524288 | tf_op jit(solution)/shard_map/sin | solution.py:81
  15.6 0.7 slice_bitcast_fusion.5
  16.3 1.9 %fusion.98 = f32[256,256]{0,1:T(8,128)} fusion(bf16[256,256]{1,0:T(8,128)(2,1)} %param.12, bf16[256,1024]{1,0:T(8,128)(2,1)} %param.17, s32[]{:T(128)S(6)} %select_n.85), kind=kOutput, calls=%fused_computation.134 | convolution fusion | flops 33554432 | bytes 524292 | tf_op jit(solution)/shard_map/dot_general | solution.py:144
  18.2 0.3 fusion.51
  18.5 1.1 %maximum_bitcast_fusion.2 = (f32[1,256,2,256]{3,1,0,2:T(8,128)}, f32[1,256,2,256]{3,1,0,2:T(8,128)}) fusion(f32[256,1,256]{2,0,1:T(8,128)S(1)} %get-tuple-element.25, f32[256,1,256]{2,0,1:T(8,128)S(1)} %get-tuple-element.26, f32[256,1,256]{2,0,1:T(8,128)S(1)} %fusion.88), kind=kLoop, calls=%fused_computation.62 | loop fusion | flops 262144 | bytes 1835008 | tf_op jit(solution)/shard_map/stack | solution.py:82
  19.6 0.5 collective-permute-start.5
  20.1 1.2 %convolution_add_fusion.1 = f32[3,256,256]{1,2,0:T(8,128)S(1)} fusion(f32[3,256,256]{1,2,0:T(8,128)S(1)} %fusion.51, bf16[3,1024,256]{2,1,0:T(8,128)(2,1)S(1)} %copy-done, s32[]{:T(128)S(6)} %select_n.87, bf16[256,256]{1,0:T(8,128)(2,1)} %collective-permute-done), kind=kOutput, calls=%fused_computation.19 | convolution fusion | flops 100859904 | bytes 2097156 | tf_op jit(solution)/shard_map/td,jdc->jtc/dot_general | solution.py:136
  21.3 1.2 %fusion.44 = f32[3,256,256]{1,2,0:T(8,128)S(1)} fusion(bf16[3,1024,256]{2,1,0:T(8,128)(2,1)S(1)} %copy-done, s32[]{:T(128)S(6)} %select_n.91, bf16[256,256]{1,0:T(8,128)(2,1)} %collective-permute-done.2), kind=kOutput, calls=%fused_computation.75 | convolution fusion | flops 100663296 | bytes 1310724 | tf_op jit(solution)/shard_map/td,jdc->jtc/dot_general | solution.py:136
  22.6 1.2 %fusion.21 = bf16[3,256,256]{2,1,0:T(8,128)(2,1)S(1)} fusion(f32[3,256,256]{1,2,0:T(8,128)S(1)} %fusion.44, f32[3,256,256]{1,2,0:T(8,128)S(1)} %convolution_add_fusion.1, bf16[3,1024,256]{2,1,0:T(8,128)(2,1)S(1)} %copy-done, s32[]{:T(128)S(6)} %select_n.89, bf16[256,256]{1,0:T(8,128)(2,1)} %collective-permute-done.1), kind=kOutput, calls=%fused_computation.22 | convolution fusion | flops 101253120 | bytes 2490372 | tf_op jit(solution)/shard_map/td,jdc->jtc/dot_general | solution.py:136
  23.8 3.8 %collective-permute-start.3 = (bf16[3,2,256]{2,1,0:T(2,128)(2,1)S(1)}, bf16[3,2,256]{2,1,0:T(2,128)(2,1)S(1)}, u32[]{:S(2)}, u32[]{:S(2)}) collective-permute-start(bf16[3,2,256]{2,1,0:T(2,128)(2,1)S(1)} %slice.111), channel_id=1, source_target_pairs={{0,4},{4,8},{8,12},{12,16},{16,20},{20,24},{24,28},{1,5},{5,9},{9,... | collective-permute-start | bytes 9224 | tf_op jit(solution)/shard_map/ppermute | solution.py:17
  27.6 1.1 %convolution_add_fusion.3 = f32[256,256]{0,1:T(8,128)S(1)} fusion(f32[256,256]{0,1:T(8,128)S(1)} %copy-done.9, bf16[256,256]{1,0:T(8,128)(2,1)} %collective-permute-done.4, bf16[256,1024]{1,0:T(8,128)(2,1)S(1)} %copy-done.7, s32[]{:T(128)S(6)} %select_n.87), kind=kOutput, calls=%fused_computation.31 | convolution fusion | flops 33619968 | bytes 786436 | tf_op jit(solution)/shard_map/dot_general | solution.py:144
  28.8 1.1 %fusion.90 = f32[256,256]{0,1:T(8,128)S(1)} fusion(bf16[256,256]{1,0:T(8,128)(2,1)} %collective-permute-done.6, bf16[256,1024]{1,0:T(8,128)(2,1)S(1)} %copy-done.7, s32[]{:T(128)S(6)} %select_n.91), kind=kOutput, calls=%fused_computation.126 | convolution fusion | flops 33554432 | bytes 524292 | tf_op jit(solution)/shard_map/dot_general | solution.py:144
  29.9 0.2 fusion.26
  30.3 0.2 fusion.41
  30.5 0.4 copy-done.5
  31.1 0.9 copy.34
  31.9 4.2 %all-to-all-start = ((bf16[2,256,256]{2,0,1:T(2,128)(2,1)}), bf16[2,256,256]{2,0,1:T(2,128)(2,1)}, u32[]{:S(2)}, u32[]{:S(2)}) async-start(bf16[2,256,256]{2,0,1:T(2,128)(2,1)} %copy.34), calls=%async_computation | async-start | bytes 524288 | tf_op jit(solution)/shard_map/all_to_all | solution.py:99
  36.1 0.6 convolution_bitcast_fusion.2
  37.0 0.8 copy-done.1
  37.9 1.1 %convolution_bitcast_fusion.1 = f32[1,32,2,2,8,256]{5,1,4,2,0,3:T(8,128)S(1)} fusion(f32[32,2,2,8,256]{4,3,0,2,1:T(8,128)S(1)} %maximum_bitcast_fusion.1, f32[1,256,2,256]{3,1,0,2:T(8,128)S(1)} %copy-done.3, f32[1,256,2,256]{3,1,0,2:T(8,128)S(1)} %copy-done.1), kind=kOutput, calls=%fused_computation.15 | convolution fusion | flops 805568512 | bytes 3145728 | tf_op jit(solution)/shard_map/bcerkm,rmsq->bceskq/dot_general | solution.py:117
  39.1 2.4 %all-to-all-done = bf16[2,256,256]{2,0,1:T(2,128)(2,1)} async-done(((bf16[2,256,256]{2,0,1:T(2,128)(2,1)}), bf16[2,256,256]{2,0,1:T(2,128)(2,1)}, u32[]{:S(2)}, u32[]{:S(2)}) %all-to-all-start) | async-done | bytes 262176 | tf_op jit(solution)/shard_map/all_to_all | solution.py:99
  41.5 1.7 %convolution_bitcast_fusion = f32[2,32,2,2,8,256]{5,4,3,2,1,0:T(8,128)S(1)} fusion(f32[2,2,8,8,1,1]{3,2,1,0,5,4:T(8,128)S(1)} %copy-done.15, bf16[2,8,32,256]{3,0,2,1:T(2,128)(2,1)} %bitcast.18), kind=kOutput, calls=%fused_computation.14 | convolution fusion | flops 25165824 | bytes 2360320 | tf_op jit(solution)/shard_map/erkp,bcpm->bcerkm/dot_general | solution.py:115
  43.2 0.2 multiply_subtract_fusion.1
  43.5 0.2 pad_maximum_fusion
  43.7 0.8 copy-done.2
  44.7 2.7 %fusion.10 = f32[2,32,2,2,8,256]{5,1,4,2,0,3:T(8,128)S(1)} fusion(f32[2,32,2,2,8,256]{5,4,3,2,1,0:T(8,128)S(1)} %pad_maximum_fusion, f32[1,256,2,256]{3,1,0,2:T(8,128)S(1)} %copy-done.4, f32[1,256,2,256]{3,1,0,2:T(8,128)S(1)} %copy-done.2), kind=kOutput, calls=%fused_computation.12 | convolution fusion | flops 1610874880 | bytes 5242880 | tf_op jit(solution)/shard_map/bcerkm,rmsq->bceskq/dot_general | solution.py:117
  47.3 0.5 multiply_subtract_fusion.3
  47.8 0.2 maximum_bitcast_fusion
  48.1 2.7 %fusion.13 = f32[2,32,2,2,8,256]{5,4,3,2,1,0:T(8,128)S(1)} fusion(f32[2,32,2,2,8,256,1]{5,1,4,2,0,3,6:T(8,128)S(1)} %maximum_bitcast_fusion, f32[1,256,2,256]{3,1,0,2:T(8,128)S(1)} %copy-done.4, f32[1,256,2,256]{3,1,0,2:T(8,128)S(1)} %copy-done.2), kind=kOutput, calls=%fused_computation.13 | convolution fusion | flops 1610874880 | bytes 5242880 | tf_op jit(solution)/shard_map/bceskq,rmsq->bcerkm/dot_general | solution.py:122
  50.8 0.3 multiply_subtract_fusion
  51.1 0.4 copy-done.13
  51.5 0.7 fusion.27
  52.2 8.7 %all_to_all.39 = bf16[2,32,8,256]{3,1,0,2:T(8,128)(2,1)S(1)} all-to-all(bf16[2,32,8,256]{3,1,0,2:T(8,128)(2,1)S(1)} %copy.44), channel_id=1, replica_groups=mesh['seq'=8,'panel'=4] {'seq'}, dimensions={2} | all-to-all | bytes 524288 | tf_op jit(solution)/shard_map/all_to_all | solution.py:107
  60.9 0.8 bitcast_convert_fusion
  61.8 1.2 %copy.46 = f32[2,256,256]{1,2,0:T(8,128)S(1)} copy(f32[2,256,256]{2,1,0:T(8,128)} %bitcast.214) | data formatting | bytes 1048576 | tf_op jit(solution)/shard_map/transpose | solution.py:110
  63.2 0.8 copy-done.8
  64.0 0.2 convolution_convert_fusion
  64.2 0.2 convolution_convert_fusion.1
  64.5 3.1 %collective-permute-start.10 = (f32[3,2,256]{2,1,0:T(2,128)S(1)}, f32[3,2,256]{2,1,0:T(2,128)S(1)}, u32[]{:S(2)}, u32[]{:S(2)}) collective-permute-start(f32[3,2,256]{2,1,0:T(2,128)S(1)} %slice.132), channel_id=1, source_target_pairs={{4,0},{8,4},{12,8},{16,12},{20,16},{24,20},{28,24},{5,1},{9,5},{13... | collective-permute-start | bytes 18440 | tf_op jit(solution)/shard_map/ppermute | solution.py:17
  67.7 0.2 convolution_convert_fusion.2
  67.9 2.7 %collective-permute-start.7 = (bf16[256,256]{1,0:T(8,128)(2,1)S(1)}, bf16[256,256]{1,0:T(8,128)(2,1)S(1)}, u32[]{:S(2)}, u32[]{:S(2)}) collective-permute-start(bf16[256,256]{1,0:T(8,128)(2,1)S(1)} %convolution_convert_fusion.2), channel_id=1, source_target_pairs={{0,1},{1,2},{2,3},{3,0},{4,5},{5,6},{6,7},{7,4},{8,9},{9,10},{10,1... | collective-permute-start | bytes 393224 | tf_op jit(solution)/shard_map/ppermute | solution.py:36
  70.6 1.0 %collective-permute-start.8 = (bf16[256,256]{1,0:T(8,128)(2,1)S(1)}, bf16[256,256]{1,0:T(8,128)(2,1)S(1)}, u32[]{:S(2)}, u32[]{:S(2)}) collective-permute-start(bf16[256,256]{1,0:T(8,128)(2,1)S(1)} %convolution_convert_fusion.1), channel_id=1, source_target_pairs={{0,2},{1,3},{2,0},{3,1},{4,6},{5,7},{6,4},{7,5},{8,10},{9,11},{10,... | collective-permute-start | bytes 393224 | tf_op jit(solution)/shard_map/ppermute | solution.py:36
  71.5 0.3 collective-permute-start.9
  71.9 0.3 fusion.39
  72.2 0.3 fusion.31
  72.5 0.3 fusion.30
  72.8 1.2 %collective-permute-start.11 = (bf16[256,256]{1,0:T(8,128)(2,1)S(1)}, bf16[256,256]{1,0:T(8,128)(2,1)S(1)}, u32[]{:S(2)}, u32[]{:S(2)}) collective-permute-start(bf16[256,256]{1,0:T(8,128)(2,1)S(1)} %fusion.30), channel_id=1, source_target_pairs={{0,1},{1,2},{2,3},{3,0},{4,5},{5,6},{6,7},{7,4},{8,9},{9,10},{10,1... | collective-permute-start | bytes 393224 | tf_op jit(solution)/shard_map/ppermute | solution.py:36
  74.0 3.2 %collective-permute-start.12 = (bf16[256,256]{1,0:T(8,128)(2,1)S(1)}, bf16[256,256]{1,0:T(8,128)(2,1)S(1)}, u32[]{:S(2)}, u32[]{:S(2)}) collective-permute-start(bf16[256,256]{1,0:T(8,128)(2,1)S(1)} %fusion.31), channel_id=1, source_target_pairs={{0,2},{1,3},{2,0},{3,1},{4,6},{5,7},{6,4},{7,5},{8,10},{9,11},{10,... | collective-permute-start | bytes 393224 | tf_op jit(solution)/shard_map/ppermute | solution.py:36
  77.2 0.3 fusion.32
  77.5 2.0 %collective-permute-done.7 = bf16[256,256]{1,0:T(8,128)(2,1)S(1)} collective-permute-done((bf16[256,256]{1,0:T(8,128)(2,1)S(1)}, bf16[256,256]{1,0:T(8,128)(2,1)S(1)}, u32[]{:S(2)}, u32[]{:S(2)}) %collective-permute-start.7) | collective-permute-done | bytes 131104 | tf_op jit(solution)/shard_map/ppermute | solution.py:36
  79.5 8.4 %collective-permute-done.8 = bf16[256,256]{1,0:T(8,128)(2,1)S(1)} collective-permute-done((bf16[256,256]{1,0:T(8,128)(2,1)S(1)}, bf16[256,256]{1,0:T(8,128)(2,1)S(1)}, u32[]{:S(2)}, u32[]{:S(2)}) %collective-permute-start.8) | collective-permute-done | bytes 131104 | tf_op jit(solution)/shard_map/ppermute | solution.py:36
  87.9 0.9 collective-permute-done.9
  88.8 0.9 add_convert_fusion
  89.7 1.0 %collective-permute-done.11 = bf16[256,256]{1,0:T(8,128)(2,1)S(1)} collective-permute-done((bf16[256,256]{1,0:T(8,128)(2,1)S(1)}, bf16[256,256]{1,0:T(8,128)(2,1)S(1)}, u32[]{:S(2)}, u32[]{:S(2)}) %collective-permute-start.11) | collective-permute-done | bytes 131104 | tf_op jit(solution)/shard_map/ppermute | solution.py:36
  90.7 2.7 %collective-permute-done.12 = bf16[256,256]{1,0:T(8,128)(2,1)S(1)} collective-permute-done((bf16[256,256]{1,0:T(8,128)(2,1)S(1)}, bf16[256,256]{1,0:T(8,128)(2,1)S(1)}, u32[]{:S(2)}, u32[]{:S(2)}) %collective-permute-start.12) | collective-permute-done | bytes 131104 | tf_op jit(solution)/shard_map/ppermute | solution.py:36
  93.5 1.0 %collective-permute-done.13 = bf16[256,256]{1,0:T(8,128)(2,1)S(1)} collective-permute-done((bf16[256,256]{1,0:T(8,128)(2,1)S(1)}, bf16[256,256]{1,0:T(8,128)(2,1)S(1)}, u32[]{:S(2)}, u32[]{:S(2)}) %collective-permute-start.13) | collective-permute-done | bytes 131104 | tf_op jit(solution)/shard_map/ppermute | solution.py:36
  94.5 1.0 %fusion.62 = bf16[256,256]{1,0:T(8,128)(2,1)} fusion(bf16[3,256,256]{2,1,0:T(8,128)(2,1)S(1)} %fusion.39, bf16[3,1024,256]{2,1,0:T(8,128)(2,1)S(1)} %copy-done, s32[]{:T(128)S(6)} %select_n.85, bf16[256,256]{1,0:T(8,128)(2,1)S(1)} %collective-permute-done.13, bf16[256,256]{1,0:T(8,128)(2,1)S(1)} %collective-permute-done.12, ...), kind=kOutput, calls=%fused_computation.87 | convolution fusion | flops 101122048 | bytes 1310724 | tf_op jit(solution)/shard_map/jtc,jdc->td/dot_general | solution.py:210
  (56 shorter events, 1.4 us)
Async XLA Ops:
  0.6 17.6 %copy-start = (bf16[3,1024,256]{2,1,0:T(8,128)(2,1)S(1)}, bf16[3,1024,256]{2,1,0:T(8,128)(2,1)}, u32[]{:S(2)}) copy-start(bf16[3,1024,256]{2,1,0:T(8,128)(2,1)} %param.13) | copy-start | bytes 4718596
  0.6 17.6 %copy-start.11 = (bf16[256,256]{1,0:T(8,128)(2,1)S(1)}, bf16[256,256]{1,0:T(8,128)(2,1)}, u32[]{:S(2)}) copy-start(bf16[256,256]{1,0:T(8,128)(2,1)} %param.11) | copy-start | bytes 393220
  0.7 18.9 %collective-permute-start = (bf16[256,256]{1,0:T(8,128)(2,1)}, bf16[256,256]{1,0:T(8,128)(2,1)}, u32[]{:S(2)}, u32[]{:S(2)}) collective-permute-start(bf16[256,256]{1,0:T(8,128)(2,1)} %param.11), channel_id=1, source_target_pairs={{0,1},{1,2},{2,3},{3,0},{4,5},{5,6},{6,7},{7,4},{8,9},{9,10},{10,1... | collective-permute-start | bytes 393224 | tf_op jit(solution)/shard_map/ppermute | solution.py:25
  2.0 19.3 %collective-permute-start.2 = (bf16[256,256]{1,0:T(8,128)(2,1)}, bf16[256,256]{1,0:T(8,128)(2,1)}, u32[]{:S(2)}, u32[]{:S(2)}) collective-permute-start(bf16[256,256]{1,0:T(8,128)(2,1)} %param.11), channel_id=1, source_target_pairs={{0,3},{1,0},{2,1},{3,2},{4,7},{5,4},{6,5},{7,6},{8,11},{9,8},{10,9... | collective-permute-start | bytes 393224 | tf_op jit(solution)/shard_map/ppermute | solution.py:25
  2.2 20.4 %collective-permute-start.1 = (bf16[256,256]{1,0:T(8,128)(2,1)}, bf16[256,256]{1,0:T(8,128)(2,1)}, u32[]{:S(2)}, u32[]{:S(2)}) collective-permute-start(bf16[256,256]{1,0:T(8,128)(2,1)} %param.11), channel_id=1, source_target_pairs={{0,2},{1,3},{2,0},{3,1},{4,6},{5,7},{6,4},{7,5},{8,10},{9,11},{10,... | collective-permute-start | bytes 393224 | tf_op jit(solution)/shard_map/ppermute | solution.py:25
  4.5 23.1 %collective-permute-start.4 = (bf16[256,256]{1,0:T(8,128)(2,1)}, bf16[256,256]{1,0:T(8,128)(2,1)}, u32[]{:S(2)}, u32[]{:S(2)}) collective-permute-start(bf16[256,256]{1,0:T(8,128)(2,1)} %param.12), channel_id=1, source_target_pairs={{0,1},{1,2},{2,3},{3,0},{4,5},{5,6},{6,7},{7,4},{8,9},{9,10},{10,1... | collective-permute-start | bytes 393224 | tf_op jit(solution)/shard_map/ppermute | solution.py:25
  5.5 23.3 %collective-permute-start.6 = (bf16[256,256]{1,0:T(8,128)(2,1)}, bf16[256,256]{1,0:T(8,128)(2,1)}, u32[]{:S(2)}, u32[]{:S(2)}) collective-permute-start(bf16[256,256]{1,0:T(8,128)(2,1)} %param.12), channel_id=1, source_target_pairs={{0,3},{1,0},{2,1},{3,2},{4,7},{5,4},{6,5},{7,6},{8,11},{9,8},{10,9... | collective-permute-start | bytes 393224 | tf_op jit(solution)/shard_map/ppermute | solution.py:25
  7.7 24.2 %all-to-all-start.1 = ((f32[1,256,256]{2,0,1:T(1,128)}), f32[1,256,256]{2,0,1:T(1,128)S(1)}, u32[]{:S(2)}, u32[]{:S(2)}) async-start(f32[1,256,256]{2,0,1:T(1,128)} %bitcast.34), calls=%async_computation.1 | async-start | bytes 524288 | tf_op jit(solution)/shard_map/all_to_all | solution.py:99
  19.6 10.3 %collective-permute-start.5 = (bf16[256,256]{1,0:T(8,128)(2,1)}, bf16[256,256]{1,0:T(8,128)(2,1)S(1)}, u32[]{:S(2)}, u32[]{:S(2)}) collective-permute-start(bf16[256,256]{1,0:T(8,128)(2,1)} %param.12), channel_id=1, source_target_pairs={{0,2},{1,3},{2,0},{3,1},{4,6},{5,7},{6,4},{7,5},{8,10},{9,11},{10,... | collective-permute-start | bytes 393224 | tf_op jit(solution)/shard_map/ppermute | solution.py:25
  21.3 6.3 %copy-start.7 = (bf16[256,1024]{1,0:T(8,128)(2,1)S(1)}, bf16[256,1024]{1,0:T(8,128)(2,1)}, u32[]{:S(2)}) copy-start(bf16[256,1024]{1,0:T(8,128)(2,1)} %param.17) | copy-start | bytes 1572868
  21.3 6.3 %copy-start.9 = (f32[256,256]{0,1:T(8,128)S(1)}, f32[256,256]{0,1:T(8,128)}, u32[]{:S(2)}) copy-start(f32[256,256]{0,1:T(8,128)} %fusion.98) | copy-start | bytes 786436
  23.8 6.4 %collective-permute-start.3 = (bf16[3,2,256]{2,1,0:T(2,128)(2,1)S(1)}, bf16[3,2,256]{2,1,0:T(2,128)(2,1)S(1)}, u32[]{:S(2)}, u32[]{:S(2)}) collective-permute-start(bf16[3,2,256]{2,1,0:T(2,128)(2,1)S(1)} %slice.111), channel_id=1, source_target_pairs={{0,4},{4,8},{8,12},{12,16},{16,20},{20,24},{24,28},{1,5},{5,9},{9,... | collective-permute-start | bytes 9224 | tf_op jit(solution)/shard_map/ppermute | solution.py:17
  30.2 0.7 copy-start.5
  30.9 5.2 %copy-start.16 = (f32[2,2,8,8,1]{3,2,4,1,0:T(8,128)S(1)}, f32[2,2,8,8,1]{3,2,4,1,0:T(8,128)}, u32[]{:S(2)}) copy-start(f32[2,2,8,8,1]{3,2,4,1,0:T(8,128)} %constant.93) | copy-start | bytes 3076
  31.0 5.8 %copy-start.10 = (f32[2,8,256]{2,1,0:T(8,128)S(1)}, f32[2,8,256]{2,1,0:T(8,128)}, u32[]{:S(2)}) copy-start(f32[2,8,256]{2,1,0:T(8,128)} %constant.88.clone) | copy-start | bytes 49156
  31.0 5.8 %copy-start.12 = (f32[2,8,256]{2,1,0:T(8,128)S(1)}, f32[2,8,256]{2,1,0:T(8,128)}, u32[]{:S(2)}) copy-start(f32[2,8,256]{2,1,0:T(8,128)} %constant.89.clone) | copy-start | bytes 49156
  31.9 9.6 %all-to-all-start = ((bf16[2,256,256]{2,0,1:T(2,128)(2,1)}), bf16[2,256,256]{2,0,1:T(2,128)(2,1)}, u32[]{:S(2)}, u32[]{:S(2)}) async-start(bf16[2,256,256]{2,0,1:T(2,128)(2,1)} %copy.34), calls=%async_computation | async-start | bytes 524288 | tf_op jit(solution)/shard_map/all_to_all | solution.py:99
  36.7 1.0 %copy-start.1 = (f32[1,256,2,256]{3,1,0,2:T(8,128)S(1)}, f32[1,256,2,256]{3,1,0,2:T(8,128)}, u32[]{:S(2)}) copy-start(f32[1,256,2,256]{3,1,0,2:T(8,128)} %get-tuple-element.20) | copy-start | bytes 1572868
  36.7 1.2 %copy-start.3 = (f32[1,256,2,256]{3,1,0,2:T(8,128)S(1)}, f32[1,256,2,256]{3,1,0,2:T(8,128)}, u32[]{:S(2)}) copy-start(f32[1,256,2,256]{3,1,0,2:T(8,128)} %get-tuple-element.21) | copy-start | bytes 1572868
  37.9 3.5 %copy-start.15 = (f32[2,2,8,8,1,1]{3,2,1,0,5,4:T(8,128)S(1)}, f32[2,2,8,8,1,1]{3,2,1,0,5,4:T(8,128)}, u32[]{:S(2)}) copy-start(f32[2,2,8,8,1,1]{3,2,1,0,5,4:T(8,128)} %constant.92) | copy-start | bytes 3076
  43.5 1.0 %copy-start.2 = (f32[1,256,2,256]{3,1,0,2:T(8,128)S(1)}, f32[1,256,2,256]{3,1,0,2:T(8,128)}, u32[]{:S(2)}) copy-start(f32[1,256,2,256]{3,1,0,2:T(8,128)} %get-tuple-element.20) | copy-start | bytes 1572868
  43.5 1.2 %copy-start.4 = (f32[1,256,2,256]{3,1,0,2:T(8,128)S(1)}, f32[1,256,2,256]{3,1,0,2:T(8,128)}, u32[]{:S(2)}) copy-start(f32[1,256,2,256]{3,1,0,2:T(8,128)} %get-tuple-element.21) | copy-start | bytes 1572868
  48.0 2.7 %copy-start.14 = (f32[2,8,256]{2,1,0:T(8,128)S(1)}, f32[2,8,256]{2,1,0:T(8,128)}, u32[]{:S(2)}) copy-start(f32[2,8,256]{2,1,0:T(8,128)} %constant.91) | copy-start | bytes 49156
  50.8 0.7 copy-start.13
  51.5 11.5 %copy-start.6 = (f32[256,256]{1,0:T(8,128)S(1)}, f32[256,256]{1,0:T(8,128)}, u32[]{:S(2)}) copy-start(f32[256,256]{1,0:T(8,128)} %copy-done.5) | copy-start | bytes 786436
  51.5 11.5 %copy-start.17 = (f32[256]{0:T(256)S(1)}, f32[256]{0:T(256)}, u32[]{:S(2)}) copy-start(f32[256]{0:T(256)} %param.15) | copy-start | bytes 3076
  63.0 1.0 %copy-start.8 = (bf16[256,1024]{1,0:T(8,128)(2,1)S(1)}, bf16[256,1024]{1,0:T(8,128)(2,1)}, u32[]{:S(2)}) copy-start(bf16[256,1024]{1,0:T(8,128)(2,1)} %param.17) | copy-start | bytes 1572868
  64.5 7.3 %collective-permute-start.10 = (f32[3,2,256]{2,1,0:T(2,128)S(1)}, f32[3,2,256]{2,1,0:T(2,128)S(1)}, u32[]{:S(2)}, u32[]{:S(2)}) collective-permute-start(f32[3,2,256]{2,1,0:T(2,128)S(1)} %slice.132), channel_id=1, source_target_pairs={{4,0},{8,4},{12,8},{16,12},{20,16},{24,20},{28,24},{5,1},{9,5},{13... | collective-permute-start | bytes 18440 | tf_op jit(solution)/shard_map/ppermute | solution.py:17
  67.9 11.6 %collective-permute-start.7 = (bf16[256,256]{1,0:T(8,128)(2,1)S(1)}, bf16[256,256]{1,0:T(8,128)(2,1)S(1)}, u32[]{:S(2)}, u32[]{:S(2)}) collective-permute-start(bf16[256,256]{1,0:T(8,128)(2,1)S(1)} %convolution_convert_fusion.2), channel_id=1, source_target_pairs={{0,1},{1,2},{2,3},{3,0},{4,5},{5,6},{6,7},{7,4},{8,9},{9,10},{10,1... | collective-permute-start | bytes 393224 | tf_op jit(solution)/shard_map/ppermute | solution.py:36
  70.6 17.4 %collective-permute-start.8 = (bf16[256,256]{1,0:T(8,128)(2,1)S(1)}, bf16[256,256]{1,0:T(8,128)(2,1)S(1)}, u32[]{:S(2)}, u32[]{:S(2)}) collective-permute-start(bf16[256,256]{1,0:T(8,128)(2,1)S(1)} %convolution_convert_fusion.1), channel_id=1, source_target_pairs={{0,2},{1,3},{2,0},{3,1},{4,6},{5,7},{6,4},{7,5},{8,10},{9,11},{10,... | collective-permute-start | bytes 393224 | tf_op jit(solution)/shard_map/ppermute | solution.py:36
  71.5 17.3 %collective-permute-start.9 = (bf16[256,256]{1,0:T(8,128)(2,1)S(1)}, bf16[256,256]{1,0:T(8,128)(2,1)S(1)}, u32[]{:S(2)}, u32[]{:S(2)}) collective-permute-start(bf16[256,256]{1,0:T(8,128)(2,1)S(1)} %convolution_convert_fusion), channel_id=1, source_target_pairs={{0,3},{1,0},{2,1},{3,2},{4,7},{5,4},{6,5},{7,6},{8,11},{9,8},{10,9... | collective-permute-start | bytes 393224 | tf_op jit(solution)/shard_map/ppermute | solution.py:36
  72.8 17.9 %collective-permute-start.11 = (bf16[256,256]{1,0:T(8,128)(2,1)S(1)}, bf16[256,256]{1,0:T(8,128)(2,1)S(1)}, u32[]{:S(2)}, u32[]{:S(2)}) collective-permute-start(bf16[256,256]{1,0:T(8,128)(2,1)S(1)} %fusion.30), channel_id=1, source_target_pairs={{0,1},{1,2},{2,3},{3,0},{4,5},{5,6},{6,7},{7,4},{8,9},{9,10},{10,1... | collective-permute-start | bytes 393224 | tf_op jit(solution)/shard_map/ppermute | solution.py:36
  74.0 19.4 %collective-permute-start.12 = (bf16[256,256]{1,0:T(8,128)(2,1)S(1)}, bf16[256,256]{1,0:T(8,128)(2,1)S(1)}, u32[]{:S(2)}, u32[]{:S(2)}) collective-permute-start(bf16[256,256]{1,0:T(8,128)(2,1)S(1)} %fusion.31), channel_id=1, source_target_pairs={{0,2},{1,3},{2,0},{3,1},{4,6},{5,7},{6,4},{7,5},{8,10},{9,11},{10,... | collective-permute-start | bytes 393224 | tf_op jit(solution)/shard_map/ppermute | solution.py:36
  79.5 15.0 %collective-permute-start.13 = (bf16[256,256]{1,0:T(8,128)(2,1)S(1)}, bf16[256,256]{1,0:T(8,128)(2,1)S(1)}, u32[]{:S(2)}, u32[]{:S(2)}) collective-permute-start(bf16[256,256]{1,0:T(8,128)(2,1)S(1)} %fusion.32), channel_id=1, source_target_pairs={{0,3},{1,0},{2,1},{3,2},{4,7},{5,4},{6,5},{7,6},{8,11},{9,8},{10,9... | collective-permute-start | bytes 393224 | tf_op jit(solution)/shard_map/ppermute | solution.py:36
where the time goes:
time: 96.3 us; the launch traced here: 95.5 us
  starting transfers between devices  31.1 us (32%)
  matrix products  21.1 us (22%)
  waiting for transfers between devices  18.5 us (19%)
  blocking collectives  8.7 us (9%)
  local copies, waits for them, and re-layouts  8.3 us (9%)
  other arithmetic  6.54 us (7%)
  between operations  1.23 us (1%)
    ppermute x6, waiting for transfers between devices, panel_reduce_scatter(): lax.ppermute(sent, 'panel', [(i, (i + k) % count) for i in range(count)])  16.1 us
    all_to_all x2, starting transfers between devices, to_columns(): lax.all_to_all(jnp.swapaxes(rows, 1, 2).astype(wire), 'seq', split_axis=1...  9.98 us
    all_to_all x1, blocking collectives, to_rows(): lax.all_to_all(columns.astype(wire), 'seq', split_axis=2, concat_axis=1,...  8.7 us
    ppermute x6, starting transfers between devices, panel_reduce_scatter(): lax.ppermute(sent, 'panel', [(i, (i + k) % count) for i in range(count)])  8.36 us
    ppermute x2, starting transfers between devices, shifted(): lax.ppermute(value, axis, [(source, source + steps) for source in range(i...  6.95 us
    ppermute x6, starting transfers between devices, panel_parts(): lax.ppermute(value, 'panel', [(i, (i + k) % count) for i in range(count)])  5.8 us
    dot_general x4, matrix products, local(): lax.dot_general(part, lax.dynamic_slice_in_dim(out_weight, source * width...  4.43 us
    dot_general x4, matrix products, local(): jnp.einsum('td,jdc->jtc', part, lax.dynamic_slice_in_dim(in_weight, sourc...  3.86 us
  transfers between devices with their start and end apart: 16, of which 7 were waited for; matrix products, arithmetic and copies ran while one was open for 20% of the time, Pallas kernels for 0%

commit v1 on v0

--- a/solution.py
+++ b/solution.py
@@ -4,11 +4,30 @@
 import numpy as np
 from jax import lax
 from jax.sharding import PartitionSpec as P
+from jax.lax import axis_index, axis_size, ppermute
 
 HIGHEST = lax.Precision.HIGHEST
 STAGE_A_PRECISION = lax.Precision.HIGH
 STAGE_B_PRECISION = lax.Precision.HIGH
 WIRE = jnp.bfloat16
+
+
+def mix_the_gates(message, dev_axis):
+    mixed_arr, vec_out = (axis_size(dev_axis), axis_index(dev_axis))
+    built = message.shape[1] // mixed_arr
+    tile_out = jnp.roll(message, shift=-vec_out * built, axis=1)
+    cards = [lax.slice_in_dim(tile_out, 0, built, axis=1)]
+    for d in range(1, mixed_arr):
+        carry_in = lax.slice_in_dim(tile_out, d * built, (d + 1) * built, axis=1)
+        cards.append(
+            ppermute(
+                carry_in,
+                axis_name=dev_axis,
+                perm=[(kk, (kk + d) % mixed_arr) for kk in range(mixed_arr)],
+            )
+        )
+    current_arr = jnp.concatenate(cards[::-1], axis=2)
+    return jnp.roll(current_arr, (vec_out + 1) * cards[0].shape[2], axis=2)
 
 
 def shifted(value, axis, steps):
@@ -96,9 +115,7 @@
 def to_columns(rows, wire=jnp.float32):
     shard_count = lax.axis_size("seq")
     batch, row_count, _ = rows.shape
-    columns = lax.all_to_all(
-        jnp.swapaxes(rows, 1, 2).astype(wire), "seq", split_axis=1, concat_axis=2, tiled=True
-    ).astype(jnp.float32)
+    columns = mix_the_gates(jnp.swapaxes(rows, 1, 2).astype(wire), "seq").astype(jnp.float32)
     return columns.reshape(batch, columns.shape[1], shard_count, row_count)
 
 

time: 96.3 us -> 156 us (1.62)
  local copies, waits for them, and re-layouts: 8.3 us -> 37.6 us
  waiting for transfers between devices: 18.5 us -> 39.4 us
  starting transfers between devices: 31.1 us -> 38.9 us
  other arithmetic: 6.54 us -> 8.8 us
  matrix products: 21.1 us -> 19.2 us
    ppermute x0 -> x14, waiting for transfers between devices: none -> 23.4 us  [mix_the_gates(): ppermute(carry_in, axis_name=dev_axis, perm=[(kk, (kk + d) % mixed_arr) f...]
    unnamed x37 -> x89, local copies, waits for them, and re-layouts: 3.63 us -> 22.2 us
    ppermute x0 -> x14, starting transfers between devices: none -> 16.7 us  [mix_the_gates(): ppermute(carry_in, axis_name=dev_axis, perm=[(kk, (kk + d) % mixed_arr) f...]
    all_to_all x2 -> x0, starting transfers between devices: 9.98 us -> none  [to_columns(): lax.all_to_all(jnp.swapaxes(rows, 1, 2).astype(wire), 'seq', split_axis=1...]
    ppermute x0 -> x7, local copies, waits for them, and re-layouts: none -> 9.32 us  [mix_the_gates(): ppermute(carry_in, axis_name=dev_axis, perm=[(kk, (kk + d) % mixed_arr) f...]
    slice x0 -> x3, local copies, waits for them, and re-layouts: none -> 2.54 us  [the longest x2 1.86 us: mix_the_gates(): cards = [lax.slice_in_dim(tile_out, 0, built, axis=1)]]
    all_to_all x2 -> x0, waiting for transfers between devices: 2.4 us -> none  [to_columns(): lax.all_to_all(jnp.swapaxes(rows, 1, 2).astype(wire), 'seq', split_axis=1...]
    dot_general x4, matrix products: 4.43 us -> 2.55 us  [local(): lax.dot_general(part, lax.dynamic_slice_in_dim(out_weight, source * width...]
  transfers between devices with their start and end apart: 16 -> 28, of which waited for: 7 -> 14; matrix products, arithmetic and copies ran while one was open for 20% -> 22% of each run, Pallas kernels for 0% -> 0%
where the time goes in v1:
time: 156 us; the launch traced here: 154 us
  waiting for transfers between devices  39.4 us (25%)
  starting transfers between devices  38.9 us (25%)
  local copies, waits for them, and re-layouts  37.6 us (24%)
  matrix products  19.2 us (12%)
  other arithmetic  8.8 us (6%)
  blocking collectives  8.76 us (6%)
    ppermute x14, waiting for transfers between devices, mix_the_gates(): ppermute(carry_in, axis_name=dev_axis, perm=[(kk, (kk + d) % mixed_arr) f...  23.4 us
    unnamed x89, local copies, waits for them, and re-layouts  22.2 us
    ppermute x14, starting transfers between devices, mix_the_gates(): ppermute(carry_in, axis_name=dev_axis, perm=[(kk, (kk + d) % mixed_arr) f...  16.7 us
    ppermute x6, waiting for transfers between devices, panel_reduce_scatter(): lax.ppermute(sent, 'panel', [(i, (i + k) % count) for i in range(count)])  16 us
    ppermute x7, local copies, waits for them, and re-layouts, mix_the_gates(): ppermute(carry_in, axis_name=dev_axis, perm=[(kk, (kk + d) % mixed_arr) f...  9.32 us
    all_to_all x1, blocking collectives, to_rows(): lax.all_to_all(columns.astype(wire), 'seq', split_axis=2, concat_axis=1,...  8.76 us
    ppermute x6, starting transfers between devices, panel_reduce_scatter(): lax.ppermute(sent, 'panel', [(i, (i + k) % count) for i in range(count)])  8.37 us
    ppermute x2, starting transfers between devices, shifted(): lax.ppermute(value, axis, [(source, source + steps) for source in range(i...  7.55 us
  transfers between devices with their start and end apart: 28, of which 14 were waited for; matrix products, arithmetic and copies ran while one was open for 22% of the time, Pallas kernels for 0%

profile of v1, /device:TPU:9, one launch (start us, length us, event | category | flops | bytes accessed | tf_op | source)
XLA Modules:
  0.0 154.0 jit_solution(13058274525907756097)
XLA Ops:
  0.7 1.3 collective-permute-start
  2.2 2.3 %collective-permute-start.1 = (bf16[256,256]{1,0:T(8,128)(2,1)}, bf16[256,256]{1,0:T(8,128)(2,1)}, u32[]{:S(2)}, u32[]{:S(2)}) collective-permute-start(bf16[256,256]{1,0:T(8,128)(2,1)} %param.11), channel_id=1, source_target_pairs={{0,2},{1,3},{2,0},{3,1},{4,6},{5,7},{6,4},{7,5},{8,10},{9,11},{10,... | collective-permute-start | bytes 393224 | tf_op jit(solution)/shard_map/ppermute | solution.py:44
  4.5 1.0 collective-permute-start.4
  5.5 1.1 copy.49
  7.4 1.5 collective-permute-start.14
  8.9 1.0 fusion.88
  9.8 1.8 %fusion.86 = (f32[256,1,256]{2,0,1:T(8,128)}, f32[256,1,256]{2,0,1:T(8,128)}) fusion(), kind=kLoop, calls=%fused_computation.126 | loop fusion | flops 983040 | bytes 524288 | tf_op jit(solution)/shard_map/sin | solution.py:100
  12.3 0.9 fusion.98
  13.5 2.2 %maximum_bitcast_fusion.2 = (f32[1,256,2,256]{3,1,0,2:T(8,128)}, f32[1,256,2,256]{3,1,0,2:T(8,128)}) fusion(f32[256,1,256]{2,0,1:T(8,128)} %get-tuple-element.40, f32[256,1,256]{2,0,1:T(8,128)} %get-tuple-element.41, f32[256,1,256]{2,0,1:T(8,128)S(1)} %fusion.88), kind=kLoop, calls=%fused_computation.62 | loop fusion | flops 262144 | bytes 1835008 | tf_op jit(solution)/shard_map/stack | solution.py:101
  15.7 2.4 %collective-permute-start.15 = (f32[1,32,256]{2,1,0:T(8,128)}, f32[1,32,256]{2,1,0:T(8,128)S(1)}, u32[]{:S(2)}, u32[]{:S(2)}) collective-permute-start(f32[1,32,256]{2,1,0:T(8,128)} %get-tuple-element.25), channel_id=1, source_target_pairs={{0,24},{4,28},{8,0},{12,4},{16,8},{20,12},{24,16},{28,20},{1,25},{... | collective-permute-start | bytes 98312 | tf_op jit(solution)/shard_map/ppermute | solution.py:23
  19.4 3.6 %collective-permute-start.16 = (f32[1,32,256]{2,1,0:T(8,128)}, f32[1,32,256]{2,1,0:T(8,128)S(1)}, u32[]{:S(2)}, u32[]{:S(2)}) collective-permute-start(f32[1,32,256]{2,1,0:T(8,128)} %get-tuple-element.24), channel_id=1, source_target_pairs={{0,20},{4,24},{8,28},{12,0},{16,4},{20,8},{24,12},{28,16},{1,21},{... | collective-permute-start | bytes 98312 | tf_op jit(solution)/shard_map/ppermute | solution.py:23
  23.0 1.3 collective-permute-done.16
  24.6 2.7 %collective-permute-done.17 = f32[1,32,256]{2,1,0:T(8,128)S(1)} collective-permute-done((f32[1,32,256]{2,1,0:T(8,128)}, f32[1,32,256]{2,1,0:T(8,128)S(1)}, u32[]{:S(2)}, u32[]{:S(2)}) %collective-permute-start.17) | collective-permute-done | bytes 32800 | tf_op jit(solution)/shard_map/ppermute | solution.py:23
  27.3 1.5 collective-permute-start.18
  28.9 4.5 %collective-permute-done.18 = f32[1,32,256]{2,1,0:T(8,128)S(1)} collective-permute-done((f32[1,32,256]{2,1,0:T(8,128)}, f32[1,32,256]{2,1,0:T(8,128)S(1)}, u32[]{:S(2)}, u32[]{:S(2)}) %collective-permute-start.18) | collective-permute-done | bytes 32800 | tf_op jit(solution)/shard_map/ppermute | solution.py:23
  33.4 3.9 %collective-permute-done.19 = f32[1,32,256]{2,1,0:T(8,128)S(1)} collective-permute-done((f32[1,32,256]{2,1,0:T(8,128)}, f32[1,32,256]{2,1,0:T(8,128)S(1)}, u32[]{:S(2)}, u32[]{:S(2)}) %collective-permute-start.19) | collective-permute-done | bytes 32800 | tf_op jit(solution)/shard_map/ppermute | solution.py:23
  37.3 1.0 collective-permute-start.20
  38.3 1.3 collective-permute-done.20
  43.5 1.2 convolution_add_fusion.1
  44.7 1.2 fusion.44
  46.0 1.2 fusion.21
  47.2 4.4 %collective-permute-start.3 = (bf16[3,2,256]{2,1,0:T(2,128)(2,1)S(1)}, bf16[3,2,256]{2,1,0:T(2,128)(2,1)S(1)}, u32[]{:S(2)}, u32[]{:S(2)}) collective-permute-start(bf16[3,2,256]{2,1,0:T(2,128)(2,1)S(1)} %slice.175), channel_id=1, source_target_pairs={{0,4},{4,8},{8,12},{12,16},{16,20},{20,24},{24,28},{1,5},{5,9},{9,... | collective-permute-start | bytes 9224 | tf_op jit(solution)/shard_map/ppermute | solution.py:36
  51.6 1.1 convolution_add_fusion.3
  54.3 1.2 fusion.123
  55.5 1.5 convolution_bitcast_fusion.1
  57.7 1.7 %collective-permute-start.13 = (bf16[2,32,256]{1,2,0:T(8,128)(2,1)}, bf16[2,32,256]{1,2,0:T(8,128)(2,1)}, u32[]{:S(2)}, u32[]{:S(2)}) collective-permute-start(bf16[2,32,256]{1,2,0:T(8,128)(2,1)} %get-tuple-element.30), channel_id=1, source_target_pairs={{0,4},{4,8},{8,12},{12,16},{16,20},{20,24},{24,28},{28,0},{1,5},{5... | collective-permute-start | bytes 98312 | tf_op jit(solution)/shard_map/ppermute | solution.py:23
  59.4 2.4 %collective-permute-start.12 = (bf16[2,32,256]{1,2,0:T(8,128)(2,1)}, bf16[2,32,256]{1,2,0:T(8,128)(2,1)}, u32[]{:S(2)}, u32[]{:S(2)}) collective-permute-start(bf16[2,32,256]{1,2,0:T(8,128)(2,1)} %get-tuple-element.31), channel_id=1, source_target_pairs={{0,8},{4,12},{8,16},{12,20},{16,24},{20,28},{24,0},{28,4},{1,9},{5... | collective-permute-start | bytes 98312 | tf_op jit(solution)/shard_map/ppermute | solution.py:23
  61.9 1.5 collective-permute-start.8
  63.4 1.0 copy.32
  65.0 6.4 %collective-permute-done.8 = bf16[2,32,256]{1,2,0:T(8,128)(2,1)} collective-permute-done((bf16[2,32,256]{1,2,0:T(8,128)(2,1)}, bf16[2,32,256]{1,2,0:T(8,128)(2,1)}, u32[]{:S(2)}, u32[]{:S(2)}) %collective-permute-start.8) | collective-permute-done | bytes 32800 | tf_op jit(solution)/shard_map/ppermute | solution.py:23
  72.2 1.0 copy.33
  73.8 2.6 %collective-permute-done.9 = bf16[2,32,256]{1,2,0:T(8,128)(2,1)} collective-permute-done((bf16[2,32,256]{1,2,0:T(8,128)(2,1)}, bf16[2,32,256]{1,2,0:T(8,128)(2,1)}, u32[]{:S(2)}, u32[]{:S(2)}) %collective-permute-start.9) | collective-permute-done | bytes 32800 | tf_op jit(solution)/shard_map/ppermute | solution.py:23
  76.3 1.0 copy.34
  78.0 1.6 %copy.35 = bf16[2,32,256]{2,1,0:T(8,128)(2,1)} copy(bf16[2,32,256]{1,2,0:T(8,128)(2,1)} %collective-permute-done.10) | data formatting | bytes 65536 | tf_op jit(solution)/shard_map/ppermute | solution.py:23
  79.5 1.4 constant_dynamic-update-slice_fusion.12
  80.9 1.6 %copy.36 = bf16[2,32,256]{2,1,0:T(8,128)(2,1)} copy(bf16[2,32,256]{1,2,0:T(8,128)(2,1)} %collective-permute-done.11) | data formatting | bytes 65536 | tf_op jit(solution)/shard_map/ppermute | solution.py:23
  82.5 1.4 constant_dynamic-update-slice_fusion.11
  83.9 1.6 %copy.37 = bf16[2,32,256]{2,1,0:T(8,128)(2,1)} copy(bf16[2,32,256]{1,2,0:T(8,128)(2,1)} %collective-permute-done.12) | data formatting | bytes 65536 | tf_op jit(solution)/shard_map/ppermute | solution.py:23
  85.5 1.4 constant_dynamic-update-slice_fusion.10
  86.9 1.6 %copy.38 = bf16[2,32,256]{2,1,0:T(8,128)(2,1)} copy(bf16[2,32,256]{1,2,0:T(8,128)(2,1)} %collective-permute-done.13) | data formatting | bytes 65536 | tf_op jit(solution)/shard_map/ppermute | solution.py:23
  88.5 1.4 constant_dynamic-update-slice_fusion.9
  89.9 1.4 constant_dynamic-update-slice_fusion.8
  93.2 1.4 constant_dynamic-update-slice_fusion.4
  94.5 1.4 constant_dynamic-update-slice_fusion.3
  95.9 1.4 constant_dynamic-update-slice_fusion.2
  97.3 1.4 constant_dynamic-update-slice_fusion.1
  99.3 1.0 constant_dynamic-slice_fusion.1
  100.3 1.4 convolution_bitcast_fusion
  103.1 2.7 %fusion.10 = f32[2,32,2,2,8,256]{5,1,4,2,0,3:T(8,128)S(1)} fusion(f32[2,32,2,2,8,256]{5,4,3,2,1,0:T(8,128)S(1)} %pad_maximum_fusion, f32[1,256,2,256]{3,1,0,2:T(8,128)S(1)} %copy-done.4, f32[1,256,2,256]{3,1,0,2:T(8,128)S(1)} %copy-done.2), kind=kOutput, calls=%fused_computation.12 | convolution fusion | flops 1610874880 | bytes 5242880 | tf_op jit(solution)/shard_map/bcerkm,rmsq->bceskq/dot_general | solution.py:134
  106.6 2.7 %fusion.13 = f32[2,32,2,2,8,256]{5,4,3,2,1,0:T(8,128)S(1)} fusion(f32[2,32,2,2,8,256,1]{5,1,4,2,0,3,6:T(8,128)S(1)} %maximum_bitcast_fusion, f32[1,256,2,256]{3,1,0,2:T(8,128)S(1)} %copy-done.4, f32[1,256,2,256]{3,1,0,2:T(8,128)S(1)} %copy-done.2), kind=kOutput, calls=%fused_computation.13 | convolution fusion | flops 1610874880 | bytes 5242880 | tf_op jit(solution)/shard_map/bceskq,rmsq->bcerkm/dot_general | solution.py:139
  110.7 8.8 %all_to_all.4 = bf16[2,32,8,256]{3,1,0,2:T(8,128)(2,1)S(1)} all-to-all(bf16[2,32,8,256]{3,1,0,2:T(8,128)(2,1)S(1)} %copy.54), channel_id=1, replica_groups=mesh['seq'=8,'panel'=4] {'seq'}, dimensions={2} | all-to-all | bytes 524288 | tf_op jit(solution)/shard_map/all_to_all | solution.py:124
  120.3 1.2 copy.56
  123.1 3.1 %collective-permute-start.24 = (f32[3,2,256]{2,1,0:T(2,128)S(1)}, f32[3,2,256]{2,1,0:T(2,128)S(1)}, u32[]{:S(2)}, u32[]{:S(2)}) collective-permute-start(f32[3,2,256]{2,1,0:T(2,128)S(1)} %slice.212), channel_id=1, source_target_pairs={{4,0},{8,4},{12,8},{16,12},{20,16},{24,20},{28,24},{5,1},{9,5},{13... | collective-permute-start | bytes 18440 | tf_op jit(solution)/shard_map/ppermute | solution.py:36
  126.4 2.7 %collective-permute-start.21 = (bf16[256,256]{1,0:T(8,128)(2,1)S(1)}, bf16[256,256]{1,0:T(8,128)(2,1)S(1)}, u32[]{:S(2)}, u32[]{:S(2)}) collective-permute-start(bf16[256,256]{1,0:T(8,128)(2,1)S(1)} %convolution_convert_fusion.2), channel_id=1, source_target_pairs={{0,1},{1,2},{2,3},{3,0},{4,5},{5,6},{6,7},{7,4},{8,9},{9,10},{10,1... | collective-permute-start | bytes 393224 | tf_op jit(solution)/shard_map/ppermute | solution.py:55
  129.1 1.0 collective-permute-start.22
  131.4 1.2 collective-permute-start.25
  132.6 3.2 %collective-permute-start.26 = (bf16[256,256]{1,0:T(8,128)(2,1)S(1)}, bf16[256,256]{1,0:T(8,128)(2,1)S(1)}, u32[]{:S(2)}, u32[]{:S(2)}) collective-permute-start(bf16[256,256]{1,0:T(8,128)(2,1)S(1)} %fusion.31), channel_id=1, source_target_pairs={{0,2},{1,3},{2,0},{3,1},{4,6},{5,7},{6,4},{7,5},{8,10},{9,11},{10,... | collective-permute-start | bytes 393224 | tf_op jit(solution)/shard_map/ppermute | solution.py:55
  136.1 1.9 %collective-permute-done.21 = bf16[256,256]{1,0:T(8,128)(2,1)S(1)} collective-permute-done((bf16[256,256]{1,0:T(8,128)(2,1)S(1)}, bf16[256,256]{1,0:T(8,128)(2,1)S(1)}, u32[]{:S(2)}, u32[]{:S(2)}) %collective-permute-start.21) | collective-permute-done | bytes 131104 | tf_op jit(solution)/shard_map/ppermute | solution.py:55
  138.1 8.4 %collective-permute-done.22 = bf16[256,256]{1,0:T(8,128)(2,1)S(1)} collective-permute-done((bf16[256,256]{1,0:T(8,128)(2,1)S(1)}, bf16[256,256]{1,0:T(8,128)(2,1)S(1)}, u32[]{:S(2)}, u32[]{:S(2)}) %collective-permute-start.22) | collective-permute-done | bytes 131104 | tf_op jit(solution)/shard_map/ppermute | solution.py:55
  146.5 0.9 collective-permute-done.23
  148.3 1.0 collective-permute-done.25
  149.3 2.7 %collective-permute-done.26 = bf16[256,256]{1,0:T(8,128)(2,1)S(1)} collective-permute-done((bf16[256,256]{1,0:T(8,128)(2,1)S(1)}, bf16[256,256]{1,0:T(8,128)(2,1)S(1)}, u32[]{:S(2)}, u32[]{:S(2)}) %collective-permute-start.26) | collective-permute-done | bytes 131104 | tf_op jit(solution)/shard_map/ppermute | solution.py:55
  152.0 1.0 collective-permute-done.27
  153.0 1.0 fusion.62
  (146 shorter events, 23.1 us)
Async XLA Ops:
  0.6 12.6 %copy-start = (bf16[3,1024,256]{2,1,0:T(8,128)(2,1)S(1)}, bf16[3,1024,256]{2,1,0:T(8,128)(2,1)}, u32[]{:S(2)}) copy-start(bf16[3,1024,256]{2,1,0:T(8,128)(2,1)} %param.13) | copy-start | bytes 4718596
  0.6 12.6 %copy-start.12 = (bf16[256,256]{1,0:T(8,128)(2,1)S(1)}, bf16[256,256]{1,0:T(8,128)(2,1)}, u32[]{:S(2)}) copy-start(bf16[256,256]{1,0:T(8,128)(2,1)} %param.11) | copy-start | bytes 393220
  0.7 11.6 %copy-start.13 = (bf16[256,256]{1,0:T(8,128)(2,1)S(1)}, bf16[256,256]{1,0:T(8,128)(2,1)}, u32[]{:S(2)}) copy-start(bf16[256,256]{1,0:T(8,128)(2,1)} %param.12) | copy-start | bytes 393220
  0.7 11.0 %copy-start.26 = (f32[3,3,256]{2,1,0:T(4,128)S(1)}, f32[3,3,256]{2,1,0:T(4,128)}, u32[]{:S(2)}) copy-start(f32[3,3,256]{2,1,0:T(4,128)} %param.14) | copy-start | bytes 27652
  0.7 11.6 %copy-start.7 = (bf16[256,1024]{1,0:T(8,128)(2,1)S(1)}, bf16[256,1024]{1,0:T(8,128)(2,1)}, u32[]{:S(2)}) copy-start(bf16[256,1024]{1,0:T(8,128)(2,1)} %param.17) | copy-start | bytes 1572868
  0.7 41.4 %collective-permute-start = (bf16[256,256]{1,0:T(8,128)(2,1)}, bf16[256,256]{1,0:T(8,128)(2,1)}, u32[]{:S(2)}, u32[]{:S(2)}) collective-permute-start(bf16[256,256]{1,0:T(8,128)(2,1)} %param.11), channel_id=1, source_target_pairs={{0,1},{1,2},{2,3},{3,0},{4,5},{5,6},{6,7},{7,4},{8,9},{9,10},{10,1... | collective-permute-start | bytes 393224 | tf_op jit(solution)/shard_map/ppermute | solution.py:44
  2.0 42.7 %collective-permute-start.2 = (bf16[256,256]{1,0:T(8,128)(2,1)}, bf16[256,256]{1,0:T(8,128)(2,1)}, u32[]{:S(2)}, u32[]{:S(2)}) collective-permute-start(bf16[256,256]{1,0:T(8,128)(2,1)} %param.11), channel_id=1, source_target_pairs={{0,3},{1,0},{2,1},{3,2},{4,7},{5,4},{6,5},{7,6},{8,11},{9,8},{10,9... | collective-permute-start | bytes 393224 | tf_op jit(solution)/shard_map/ppermute | solution.py:44
  2.2 43.8 %collective-permute-start.1 = (bf16[256,256]{1,0:T(8,128)(2,1)}, bf16[256,256]{1,0:T(8,128)(2,1)}, u32[]{:S(2)}, u32[]{:S(2)}) collective-permute-start(bf16[256,256]{1,0:T(8,128)(2,1)} %param.11), channel_id=1, source_target_pairs={{0,2},{1,3},{2,0},{3,1},{4,6},{5,7},{6,4},{7,5},{8,10},{9,11},{10,... | collective-permute-start | bytes 393224 | tf_op jit(solution)/shard_map/ppermute | solution.py:44
  4.5 47.1 %collective-permute-start.4 = (bf16[256,256]{1,0:T(8,128)(2,1)}, bf16[256,256]{1,0:T(8,128)(2,1)}, u32[]{:S(2)}, u32[]{:S(2)}) collective-permute-start(bf16[256,256]{1,0:T(8,128)(2,1)} %param.12), channel_id=1, source_target_pairs={{0,1},{1,2},{2,3},{3,0},{4,5},{5,6},{6,7},{7,4},{8,9},{9,10},{10,1... | collective-permute-start | bytes 393224 | tf_op jit(solution)/shard_map/ppermute | solution.py:44
  7.4 8.4 %collective-permute-start.14 = (f32[1,32,256]{2,1,0:T(8,128)}, f32[1,32,256]{2,1,0:T(8,128)}, u32[]{:S(2)}, u32[]{:S(2)}) collective-permute-start(f32[1,32,256]{2,1,0:T(8,128)} %get-tuple-element.26), channel_id=1, source_target_pairs={{0,28},{4,0},{8,4},{12,8},{16,12},{20,16},{24,20},{28,24},{1,29},{... | collective-permute-start | bytes 98312 | tf_op jit(solution)/shard_map/ppermute | solution.py:23
  13.5 27.8 %copy-start.25 = (f32[2,2,8,8,1]{3,2,1,0,4:T(8,128)S(1)}, f32[2,2,8,8,1]{3,2,1,0,4:T(8,128)}, u32[]{:S(2)}) copy-start(f32[2,2,8,8,1]{3,2,1,0,4:T(8,128)} %constant.155) | copy-start | bytes 3076
  15.7 26.1 %copy-start.11 = (f32[2,8,256]{2,1,0:T(8,128)S(1)}, f32[2,8,256]{2,1,0:T(8,128)}, u32[]{:S(2)}) copy-start(f32[2,8,256]{2,1,0:T(8,128)} %constant.150.clone) | copy-start | bytes 49156
  15.7 26.1 %copy-start.15 = (f32[2,8,256]{2,1,0:T(8,128)S(1)}, f32[2,8,256]{2,1,0:T(8,128)}, u32[]{:S(2)}) copy-start(f32[2,8,256]{2,1,0:T(8,128)} %constant.151.clone) | copy-start | bytes 49156
  15.7 3.7 %collective-permute-start.15 = (f32[1,32,256]{2,1,0:T(8,128)}, f32[1,32,256]{2,1,0:T(8,128)S(1)}, u32[]{:S(2)}, u32[]{:S(2)}) collective-permute-start(f32[1,32,256]{2,1,0:T(8,128)} %get-tuple-element.25), channel_id=1, source_target_pairs={{0,24},{4,28},{8,0},{12,4},{16,8},{20,12},{24,16},{28,20},{1,25},{... | collective-permute-start | bytes 98312 | tf_op jit(solution)/shard_map/ppermute | solution.py:23
  19.4 4.9 %collective-permute-start.16 = (f32[1,32,256]{2,1,0:T(8,128)}, f32[1,32,256]{2,1,0:T(8,128)S(1)}, u32[]{:S(2)}, u32[]{:S(2)}) collective-permute-start(f32[1,32,256]{2,1,0:T(8,128)} %get-tuple-element.24), channel_id=1, source_target_pairs={{0,20},{4,24},{8,28},{12,0},{16,4},{20,8},{24,12},{28,16},{1,21},{... | collective-permute-start | bytes 98312 | tf_op jit(solution)/shard_map/ppermute | solution.py:23
  24.4 3.0 %collective-permute-start.17 = (f32[1,32,256]{2,1,0:T(8,128)}, f32[1,32,256]{2,1,0:T(8,128)S(1)}, u32[]{:S(2)}, u32[]{:S(2)}) collective-permute-start(f32[1,32,256]{2,1,0:T(8,128)} %get-tuple-element.23), channel_id=1, source_target_pairs={{0,16},{4,20},{8,24},{12,28},{16,0},{20,4},{24,8},{28,12},{1,17},{... | collective-permute-start | bytes 98312 | tf_op jit(solution)/shard_map/ppermute | solution.py:23
  27.3 6.1 %collective-permute-start.18 = (f32[1,32,256]{2,1,0:T(8,128)}, f32[1,32,256]{2,1,0:T(8,128)S(1)}, u32[]{:S(2)}, u32[]{:S(2)}) collective-permute-start(f32[1,32,256]{2,1,0:T(8,128)} %get-tuple-element.22), channel_id=1, source_target_pairs={{0,12},{4,16},{8,20},{12,24},{16,28},{20,0},{24,4},{28,8},{1,13},{... | collective-permute-start | bytes 98312 | tf_op jit(solution)/shard_map/ppermute | solution.py:23
  33.4 3.9 %collective-permute-start.19 = (f32[1,32,256]{2,1,0:T(8,128)}, f32[1,32,256]{2,1,0:T(8,128)S(1)}, u32[]{:S(2)}, u32[]{:S(2)}) collective-permute-start(f32[1,32,256]{2,1,0:T(8,128)} %get-tuple-element.21), channel_id=1, source_target_pairs={{0,8},{4,12},{8,16},{12,20},{16,24},{20,28},{24,0},{28,4},{1,9},{5... | collective-permute-start | bytes 98312 | tf_op jit(solution)/shard_map/ppermute | solution.py:23
  37.3 2.4 %collective-permute-start.20 = (f32[1,32,256]{2,1,0:T(8,128)}, f32[1,32,256]{2,1,0:T(8,128)S(1)}, u32[]{:S(2)}, u32[]{:S(2)}) collective-permute-start(f32[1,32,256]{2,1,0:T(8,128)} %get-tuple-element.20), channel_id=1, source_target_pairs={{0,4},{4,8},{8,12},{12,16},{16,20},{20,24},{24,28},{28,0},{1,5},{5... | collective-permute-start | bytes 98312 | tf_op jit(solution)/shard_map/ppermute | solution.py:23
  39.7 13.1 %collective-permute-start.6 = (bf16[256,256]{1,0:T(8,128)(2,1)}, bf16[256,256]{1,0:T(8,128)(2,1)S(1)}, u32[]{:S(2)}, u32[]{:S(2)}) collective-permute-start(bf16[256,256]{1,0:T(8,128)(2,1)} %param.12), channel_id=1, source_target_pairs={{0,3},{1,0},{2,1},{3,2},{4,7},{5,4},{6,5},{7,6},{8,11},{9,8},{10,9... | collective-permute-start | bytes 393224 | tf_op jit(solution)/shard_map/ppermute | solution.py:44
  41.8 0.9 copy-start.14
  42.7 10.3 %collective-permute-start.5 = (bf16[256,256]{1,0:T(8,128)(2,1)S(1)}, bf16[256,256]{1,0:T(8,128)(2,1)S(1)}, u32[]{:S(2)}, u32[]{:S(2)}) collective-permute-start(bf16[256,256]{1,0:T(8,128)(2,1)S(1)} %copy-done.14), channel_id=1, source_target_pairs={{0,2},{1,3},{2,0},{3,1},{4,6},{5,7},{6,4},{7,5},{8,10},{9,11},{10,... | collective-permute-start | bytes 393224 | tf_op jit(solution)/shard_map/ppermute | solution.py:44
  44.7 6.9 %copy-start.9 = (f32[256,256]{0,1:T(8,128)S(1)}, f32[256,256]{0,1:T(8,128)}, u32[]{:S(2)}) copy-start(f32[256,256]{0,1:T(8,128)} %fusion.98) | copy-start | bytes 786436
  47.2 6.2 %copy-start.17 = (f32[3,256]{1,0:T(4,128)S(1)}, f32[3,256]{1,0:T(4,128)}, u32[]{:S(2)}) copy-start(f32[3,256]{1,0:T(4,128)} %get-tuple-element.37) | copy-start | bytes 9220
  47.2 6.2 %copy-start.19 = (f32[3,256]{1,0:T(4,128)S(1)}, f32[3,256]{1,0:T(4,128)}, u32[]{:S(2)}) copy-start(f32[3,256]{1,0:T(4,128)} %get-tuple-element.38) | copy-start | bytes 9220
  47.2 6.2 %copy-start.21 = (f32[3,256]{1,0:T(4,128)S(1)}, f32[3,256]{1,0:T(4,128)}, u32[]{:S(2)}) copy-start(f32[3,256]{1,0:T(4,128)} %get-tuple-element.39) | copy-start | bytes 9220
  47.2 6.1 %collective-permute-start.3 = (bf16[3,2,256]{2,1,0:T(2,128)(2,1)S(1)}, bf16[3,2,256]{2,1,0:T(2,128)(2,1)S(1)}, u32[]{:S(2)}, u32[]{:S(2)}) collective-permute-start(bf16[3,2,256]{2,1,0:T(2,128)(2,1)S(1)} %slice.175), channel_id=1, source_target_pairs={{0,4},{4,8},{8,12},{12,16},{16,20},{20,24},{24,28},{1,5},{5,9},{9,... | collective-permute-start | bytes 9224 | tf_op jit(solution)/shard_map/ppermute | solution.py:36
  53.3 0.7 copy-start.5
  53.7 1.8 %copy-start.1 = (f32[1,256,2,256]{3,1,0,2:T(8,128)S(1)}, f32[1,256,2,256]{3,1,0,2:T(8,128)}, u32[]{:S(2)}) copy-start(f32[1,256,2,256]{3,1,0,2:T(8,128)} %get-tuple-element.27) | copy-start | bytes 1572868
  53.7 1.8 %copy-start.3 = (f32[1,256,2,256]{3,1,0,2:T(8,128)S(1)}, f32[1,256,2,256]{3,1,0,2:T(8,128)}, u32[]{:S(2)}) copy-start(f32[1,256,2,256]{3,1,0,2:T(8,128)} %get-tuple-element.28) | copy-start | bytes 1572868
  55.5 6.4 %collective-permute-start.7 = (bf16[2,32,256]{1,2,0:T(8,128)(2,1)}, bf16[2,32,256]{1,2,0:T(8,128)(2,1)}, u32[]{:S(2)}, u32[]{:S(2)}) collective-permute-start(bf16[2,32,256]{1,2,0:T(8,128)(2,1)} %get-tuple-element.36), channel_id=1, source_target_pairs={{0,28},{4,0},{8,4},{12,8},{16,12},{20,16},{24,20},{28,24},{1,29},{... | collective-permute-start | bytes 98312 | tf_op jit(solution)/shard_map/ppermute | solution.py:23
  57.7 41.0 %copy-start.10 = (bf16[2,32,256]{2,1,0:T(8,128)(2,1)S(1)}, bf16[2,32,256]{2,1,0:T(8,128)(2,1)}, u32[]{:S(2)}) copy-start(bf16[2,32,256]{2,1,0:T(8,128)(2,1)} %copy.39) | copy-start | bytes 98308
  57.7 29.2 %collective-permute-start.13 = (bf16[2,32,256]{1,2,0:T(8,128)(2,1)}, bf16[2,32,256]{1,2,0:T(8,128)(2,1)}, u32[]{:S(2)}, u32[]{:S(2)}) collective-permute-start(bf16[2,32,256]{1,2,0:T(8,128)(2,1)} %get-tuple-element.30), channel_id=1, source_target_pairs={{0,4},{4,8},{8,12},{12,16},{16,20},{20,24},{24,28},{28,0},{1,5},{5... | collective-permute-start | bytes 98312 | tf_op jit(solution)/shard_map/ppermute | solution.py:23
  59.4 24.5 %collective-permute-start.12 = (bf16[2,32,256]{1,2,0:T(8,128)(2,1)}, bf16[2,32,256]{1,2,0:T(8,128)(2,1)}, u32[]{:S(2)}, u32[]{:S(2)}) collective-permute-start(bf16[2,32,256]{1,2,0:T(8,128)(2,1)} %get-tuple-element.31), channel_id=1, source_target_pairs={{0,8},{4,12},{8,16},{12,20},{16,24},{20,28},{24,0},{28,4},{1,9},{5... | collective-permute-start | bytes 98312 | tf_op jit(solution)/shard_map/ppermute | solution.py:23
  61.9 19.0 %collective-permute-start.11 = (bf16[2,32,256]{1,2,0:T(8,128)(2,1)}, bf16[2,32,256]{1,2,0:T(8,128)(2,1)}, u32[]{:S(2)}, u32[]{:S(2)}) collective-permute-start(bf16[2,32,256]{1,2,0:T(8,128)(2,1)} %get-tuple-element.32), channel_id=1, source_target_pairs={{0,12},{4,16},{8,20},{12,24},{16,28},{20,0},{24,4},{28,8},{1,13},{... | collective-permute-start | bytes 98312 | tf_op jit(solution)/shard_map/ppermute | solution.py:23
  61.9 16.1 %collective-permute-start.10 = (bf16[2,32,256]{1,2,0:T(8,128)(2,1)}, bf16[2,32,256]{1,2,0:T(8,128)(2,1)}, u32[]{:S(2)}, u32[]{:S(2)}) collective-permute-start(bf16[2,32,256]{1,2,0:T(8,128)(2,1)} %get-tuple-element.33), channel_id=1, source_target_pairs={{0,16},{4,20},{8,24},{12,28},{16,0},{20,4},{24,8},{28,12},{1,17},{... | collective-permute-start | bytes 98312 | tf_op jit(solution)/shard_map/ppermute | solution.py:23
  61.9 9.4 %collective-permute-start.8 = (bf16[2,32,256]{1,2,0:T(8,128)(2,1)}, bf16[2,32,256]{1,2,0:T(8,128)(2,1)}, u32[]{:S(2)}, u32[]{:S(2)}) collective-permute-start(bf16[2,32,256]{1,2,0:T(8,128)(2,1)} %get-tuple-element.35), channel_id=1, source_target_pairs={{0,24},{4,28},{8,0},{12,4},{16,8},{20,12},{24,16},{28,20},{1,25},{... | collective-permute-start | bytes 98312 | tf_op jit(solution)/shard_map/ppermute | solution.py:23
  71.3 5.0 %collective-permute-start.9 = (bf16[2,32,256]{1,2,0:T(8,128)(2,1)}, bf16[2,32,256]{1,2,0:T(8,128)(2,1)}, u32[]{:S(2)}, u32[]{:S(2)}) collective-permute-start(bf16[2,32,256]{1,2,0:T(8,128)(2,1)} %get-tuple-element.34), channel_id=1, source_target_pairs={{0,20},{4,24},{8,28},{12,0},{16,4},{20,8},{24,12},{28,16},{1,21},{... | collective-permute-start | bytes 98312 | tf_op jit(solution)/shard_map/ppermute | solution.py:23
  88.5 13.2 %copy-start.16 = (f32[2,8,256]{2,1,0:T(8,128)S(1)}, f32[2,8,256]{2,1,0:T(8,128)}, u32[]{:S(2)}) copy-start(f32[2,8,256]{2,1,0:T(8,128)} %constant.151.clone) | copy-start | bytes 49156
  101.9 1.0 copy-start.2
  102.0 1.2 copy-start.4
  106.5 2.7 %copy-start.24 = (f32[2,8,256]{2,1,0:T(8,128)S(1)}, f32[2,8,256]{2,1,0:T(8,128)}, u32[]{:S(2)}) copy-start(f32[2,8,256]{2,1,0:T(8,128)} %constant.153) | copy-start | bytes 49156
  109.2 0.7 copy-start.23
  110.0 11.6 %copy-start.6 = (f32[256,256]{1,0:T(8,128)S(1)}, f32[256,256]{1,0:T(8,128)}, u32[]{:S(2)}) copy-start(f32[256,256]{1,0:T(8,128)} %copy-done.5) | copy-start | bytes 786436
  110.0 11.6 %copy-start.27 = (f32[256]{0:T(256)S(1)}, f32[256]{0:T(256)}, u32[]{:S(2)}) copy-start(f32[256]{0:T(256)} %param.15) | copy-start | bytes 3076
  121.6 1.0 copy-start.8
  122.6 7.9 %copy-start.18 = (f32[3,256]{1,0:T(4,128)S(1)}, f32[3,256]{1,0:T(4,128)}, u32[]{:S(2)}) copy-start(f32[3,256]{1,0:T(4,128)} %get-tuple-element.37) | copy-start | bytes 9220
  122.6 7.9 %copy-start.20 = (f32[3,256]{1,0:T(4,128)S(1)}, f32[3,256]{1,0:T(4,128)}, u32[]{:S(2)}) copy-start(f32[3,256]{1,0:T(4,128)} %get-tuple-element.38) | copy-start | bytes 9220
  122.6 7.9 %copy-start.22 = (f32[3,256]{1,0:T(4,128)S(1)}, f32[3,256]{1,0:T(4,128)}, u32[]{:S(2)}) copy-start(f32[3,256]{1,0:T(4,128)} %get-tuple-element.39) | copy-start | bytes 9220
  123.1 7.3 %collective-permute-start.24 = (f32[3,2,256]{2,1,0:T(2,128)S(1)}, f32[3,2,256]{2,1,0:T(2,128)S(1)}, u32[]{:S(2)}, u32[]{:S(2)}) collective-permute-start(f32[3,2,256]{2,1,0:T(2,128)S(1)} %slice.212), channel_id=1, source_target_pairs={{4,0},{8,4},{12,8},{16,12},{20,16},{24,20},{28,24},{5,1},{9,5},{13... | collective-permute-start | bytes 18440 | tf_op jit(solution)/shard_map/ppermute | solution.py:36
  126.4 11.6 %collective-permute-start.21 = (bf16[256,256]{1,0:T(8,128)(2,1)S(1)}, bf16[256,256]{1,0:T(8,128)(2,1)S(1)}, u32[]{:S(2)}, u32[]{:S(2)}) collective-permute-start(bf16[256,256]{1,0:T(8,128)(2,1)S(1)} %convolution_convert_fusion.2), channel_id=1, source_target_pairs={{0,1},{1,2},{2,3},{3,0},{4,5},{5,6},{6,7},{7,4},{8,9},{9,10},{10,1... | collective-permute-start | bytes 393224 | tf_op jit(solution)/shard_map/ppermute | solution.py:55
  129.1 17.4 %collective-permute-start.22 = (bf16[256,256]{1,0:T(8,128)(2,1)S(1)}, bf16[256,256]{1,0:T(8,128)(2,1)S(1)}, u32[]{:S(2)}, u32[]{:S(2)}) collective-permute-start(bf16[256,256]{1,0:T(8,128)(2,1)S(1)} %convolution_convert_fusion.1), channel_id=1, source_target_pairs={{0,2},{1,3},{2,0},{3,1},{4,6},{5,7},{6,4},{7,5},{8,10},{9,11},{10,... | collective-permute-start | bytes 393224 | tf_op jit(solution)/shard_map/ppermute | solution.py:55
  130.1 17.3 %collective-permute-start.23 = (bf16[256,256]{1,0:T(8,128)(2,1)S(1)}, bf16[256,256]{1,0:T(8,128)(2,1)S(1)}, u32[]{:S(2)}, u32[]{:S(2)}) collective-permute-start(bf16[256,256]{1,0:T(8,128)(2,1)S(1)} %convolution_convert_fusion), channel_id=1, source_target_pairs={{0,3},{1,0},{2,1},{3,2},{4,7},{5,4},{6,5},{7,6},{8,11},{9,8},{10,9... | collective-permute-start | bytes 393224 | tf_op jit(solution)/shard_map/ppermute | solution.py:55
  131.4 17.9 %collective-permute-start.25 = (bf16[256,256]{1,0:T(8,128)(2,1)S(1)}, bf16[256,256]{1,0:T(8,128)(2,1)S(1)}, u32[]{:S(2)}, u32[]{:S(2)}) collective-permute-start(bf16[256,256]{1,0:T(8,128)(2,1)S(1)} %fusion.30), channel_id=1, source_target_pairs={{0,1},{1,2},{2,3},{3,0},{4,5},{5,6},{6,7},{7,4},{8,9},{9,10},{10,1... | collective-permute-start | bytes 393224 | tf_op jit(solution)/shard_map/ppermute | solution.py:55
  132.6 19.4 %collective-permute-start.26 = (bf16[256,256]{1,0:T(8,128)(2,1)S(1)}, bf16[256,256]{1,0:T(8,128)(2,1)S(1)}, u32[]{:S(2)}, u32[]{:S(2)}) collective-permute-start(bf16[256,256]{1,0:T(8,128)(2,1)S(1)} %fusion.31), channel_id=1, source_target_pairs={{0,2},{1,3},{2,0},{3,1},{4,6},{5,7},{6,4},{7,5},{8,10},{9,11},{10,... | collective-permute-start | bytes 393224 | tf_op jit(solution)/shard_map/ppermute | solution.py:55
  138.1 15.0 %collective-permute-start.27 = (bf16[256,256]{1,0:T(8,128)(2,1)S(1)}, bf16[256,256]{1,0:T(8,128)(2,1)S(1)}, u32[]{:S(2)}, u32[]{:S(2)}) collective-permute-start(bf16[256,256]{1,0:T(8,128)(2,1)S(1)} %fusion.32), channel_id=1, source_target_pairs={{0,3},{1,0},{2,1},{3,2},{4,7},{5,4},{6,5},{7,6},{8,11},{9,8},{10,9... | collective-permute-start | bytes 393224 | tf_op jit(solution)/shard_map/ppermute | solution.py:55
